TPU v7x, 256 devices: a whole 4x4x8 slice. The times are simulated.
256 devices in a mesh: dom: 64 (over y, z, core), rep: 4 (over x).
Axes of the slice: x: 4, y: 4, z: 8, core: 2. Of those that a mesh axis runs over, the one named last changes fastest.
Arguments:
- x_loader: bfloat16 [131072, 512], P(('dom', 'rep')), may hold values from -6 to 6
- owner_index: int32 [131072], P(('dom', 'rep')), may hold values from 0 to 131071, as said below
- tile_vals: bfloat16 [1024, 12, 128, 128], P(('dom', 'rep')), as said below
- tile_cols: int32 [1024, 12], P(('dom', 'rep')), may hold values from 0 to 1023, as said below
- tile_live: int32 [1024, 12], P(('dom', 'rep')), may hold values from 0 to 1, as said below
- w_self: bfloat16 [512, 512], replicated, may hold values from -0.25 to 0.25
- w_neigh: bfloat16 [512, 512], replicated, may hold values from -3 to 3
- bias: float32 [512], replicated, may hold values from -3 to 3
- cotangent: bfloat16 [131072, 512], P(('dom', 'rep')), may hold values from -6 to 6
Outputs:
- layer_out: bfloat16 [131072, 512], P(('dom', 'rep'))
- grad_features: bfloat16 [131072, 512], P(('dom', 'rep'))
- grad_self: float32 [512, 512], replicated
- grad_neigh: float32 [512, 512], replicated
- grad_bias: float32 [512], replicated
Inputs may be any that keep to these rules, and one draw needn't show every extreme that they name: `owner_index`: A permutation of the 131072 rows. Loader rows are in blocks of 512 in the order of the devices (dom slowest); owner rows likewise. The 512 rows of each loader block with rep index r go to owner blocks of rep index r, 8 rows to each of the 64 partitions. `tile_cols`: partition p holds row tiles p * 16 to (p + 1) * 16 - 1. A column tile of a row tile of partition p lies in partition p or within 4 tiles beyond its edges. W is symmetric: every live slot (t, c) with tiles B is matched by a live slot (c, t) with tiles B^T, a slot with c = t holding a symmetric tile. `tile_live`: live slots are symmetric as stated for tile_cols. `tile_vals`: nonnegative edge weights.
All inputs are finite; a program needn't handle non-finite values.
Results may differ from a plain program's by a relative error of at most 0.0075.
Values may be sent and summed in bfloat16 or wider, within the bound.
No kernel may reach another device: no remote copies, remote signals or barrier semaphores. Data moves between devices by JAX's collectives and lax.ppermute only.
A program may use at most 64 MiB of HBM per device.

v0:
```python
import jax
import jax.numpy as jnp
from jax import lax
from jax.sharding import PartitionSpec as P

HALO_T = 4


def shifted(value, axis, steps):
    count = lax.axis_size(axis)
    first, last = (max(0, -steps), min(count, count - steps))
    return lax.ppermute(value, axis, [(source, source + steps) for source in range(first, last)])


def with_halo(block, sides, width):
    for axis, dim in sides:
        count = lax.axis_size(axis)
        forward = [(i, i + 1) for i in range(count - 1)]
        backward = [(target, source) for source, target in forward]
        low = lax.ppermute(
            lax.slice_in_dim(block, block.shape[dim] - width, None, axis=dim), axis, forward
        )
        high = lax.ppermute(lax.slice_in_dim(block, 0, width, axis=dim), axis, backward)
        block = jnp.concatenate([low, block, high], axis=dim)
    return block


def contract_rows(left, right):
    return lax.dot_general(
        left, right, (((0,), (0,)), ((), ())), preferred_element_type=jnp.float32
    )


def contract_cols(left, right):
    return lax.dot_general(
        left, right, (((1,), (1,)), ((), ())), preferred_element_type=jnp.float32
    )


def pass_rim(values, offset):
    return shifted(values.astype(jnp.bfloat16), "dom", offset).astype(values.dtype)


def shards(
    x_loader, owner_index, tile_vals, tile_cols, tile_live, w_self, w_neigh, bias, cotangent
):
    rows, width = x_loader.shape
    reps = lax.axis_size("rep")
    dom_place = lax.axis_index("dom")
    part_rows = rows * reps
    part_tiles = part_rows // 128
    row_tiles = rows // 128
    rim_rows = HALO_T * 128
    dest = owner_index // part_rows
    order = jnp.argsort(dest, stable=True)
    moved, slot = (
        lax.all_to_all(x_loader[order], "dom", split_axis=0, concat_axis=0, tiled=True),
        lax.all_to_all((owner_index % rows)[order], "dom", split_axis=0, concat_axis=0, tiled=True),
    )
    features = jnp.zeros((rows, width), jnp.bfloat16).at[slot].set(moved)
    first_tile = dom_place * part_tiles - HALO_T
    local_cols = tile_cols - first_tile
    masked = tile_vals * tile_live.astype(jnp.bfloat16)[:, :, None, None]
    degree = 1.0 + jnp.sum(masked, axis=(1, 3), dtype=jnp.float32)
    whole = lax.all_gather(features, "rep", axis=0, tiled=True)
    extended = with_halo(whole, (("dom", 0),), rim_rows)
    picked = extended.reshape(-1, 128, width)[local_cols]
    summed = jnp.einsum("tkab,tkbf->taf", masked, picked, preferred_element_type=jnp.float32)
    agg = (summed / degree[:, :, None]).reshape(rows, width).astype(jnp.bfloat16)
    pre = (
        jnp.dot(features, w_self, preferred_element_type=jnp.float32)
        + jnp.dot(agg, w_neigh, preferred_element_type=jnp.float32)
        + bias
    )
    layer_out = jnp.where(pre > 0, pre, jnp.expm1(jnp.minimum(pre, 0.0))).astype(jnp.bfloat16)
    slope = jnp.where(pre > 0, 1.0, jnp.exp(jnp.minimum(pre, 0.0)))
    dz = (cotangent.astype(jnp.float32) * slope).astype(jnp.bfloat16)
    grad_self, grad_neigh, grad_bias = lax.psum(
        (
            contract_rows(features, dz),
            contract_rows(agg, dz),
            jnp.sum(dz, axis=0, dtype=jnp.float32),
        ),
        ("dom", "rep"),
    )
    scaled = (contract_cols(dz, w_neigh) / degree.reshape(rows, 1)).astype(jnp.bfloat16)
    terms = jnp.einsum(
        "tkab,taf->tkbf",
        masked,
        scaled.reshape(row_tiles, 128, width),
        preferred_element_type=jnp.float32,
    )
    span_tiles = part_tiles + 2 * HALO_T
    selector = (
        local_cols.reshape(-1)[None, :] == jnp.arange(span_tiles, dtype=jnp.int32)[:, None]
    ).astype(jnp.float32)
    buffer = jnp.einsum(
        "en,nbf->ebf", selector, terms.reshape(-1, 128, width), precision=lax.Precision.HIGHEST
    )
    buffer = buffer.reshape(span_tiles * 128, width)
    lower = buffer[:rim_rows]
    upper = buffer[rim_rows + part_rows :]
    core = buffer[rim_rows : rim_rows + part_rows]
    core = core.at[:rim_rows].add(pass_rim(upper, 1))
    core = core.at[part_rows - rim_rows :].add(pass_rim(lower, -1))
    back = lax.psum_scatter(core, "rep", scatter_dimension=0, tiled=True)
    grad_features = (contract_cols(dz, w_self) + back).astype(jnp.bfloat16)
    return (layer_out, grad_features, grad_self, grad_neigh, grad_bias)


def solution(mesh):
    return jax.shard_map(
        shards,
        mesh=mesh,
        in_specs=(
            P(("dom", "rep"), None),
            P(("dom", "rep")),
            P(("dom", "rep"), None, None, None),
            P(("dom", "rep"), None),
            P(("dom", "rep"), None),
            P(),
            P(),
            P(),
            P(("dom", "rep"), None),
        ),
        out_specs=(P(("dom", "rep"), None), P(("dom", "rep"), None), P(), P(), P()),
        check_vma=False,
    )
```

profile of v0, /device:TPU:2, one launch (start us, length us, event | category | flops | bytes accessed | tf_op | source)
XLA Modules:
  0.0 486.7 jit_solution(7837561082085686232)
XLA Ops:
  7.2 0.8 add_select_fusion
  8.0 3.8 sort.17
  11.8 3.5 gather_fusion
  15.3 0.7 all_to_all.16
  16.0 12.1 %all-to-all-start = ((s32[64,8,1]{1,2,0:T(1,128)}), s32[64,8,1]{1,2,0:T(1,128)S(1)}, u32[]{:S(2)}, u32[]{:S(2)}) async-start(s32[64,8,1]{1,2,0:T(1,128)} %bitcast), calls=%async_computation | async-start | bytes 65536 | tf_op jit(solution)/shard_map/all_to_all | solution.py:58
  28.1 2.6 gather_fusion.1
  30.7 6.8 %all-to-all-done = s32[64,8,1]{1,2,0:T(1,128)S(1)} async-done(((s32[64,8,1]{1,2,0:T(1,128)}), s32[64,8,1]{1,2,0:T(1,128)S(1)}, u32[]{:S(2)}, u32[]{:S(2)}) %all-to-all-start) | async-done | bytes 2080 | tf_op jit(solution)/shard_map/all_to_all | solution.py:58
  37.5 4.6 all-to-all-start.1
  42.2 0.5 broadcast.92
  42.7 0.7 reduce.7
  43.5 0.1 all_to_all.18
  43.6 15.8 %all-to-all-done.1 = bf16[64,8,512]{2,1,0:T(8,128)(2,1)S(1)} async-done(((bf16[64,8,512]{2,1,0:T(8,128)(2,1)}), bf16[64,8,512]{2,1,0:T(8,128)(2,1)S(1)}, u32[]{:S(2)}, u32[]{:S(2)}) %all-to-all-start.1) | async-done | bytes 524320 | tf_op jit(solution)/shard_map/all_to_all | solution.py:57
  59.4 3.2 scatter_custom_fusion
  62.6 0.1 reshape.147
  62.7 0.5 convert_reduce_fusion
  63.2 29.2 %all-gather.2.cloned.1.call-done = bf16[2048,512]{1,0:T(8,128)(2,1)} async-done(((bf16[512,512]{1,0:T(8,128)(2,1)}), bf16[2048,512]{1,0:T(8,128)(2,1)}) %all-gather.2.cloned.1.call-update) | async-done | bytes 2097168 | tf_op jit(solution)/shard_map/all_gather | solution.py:65
  92.4 2.2 fusion.26
  94.6 2.5 collective-permute-start
  97.2 1.3 collective-permute-start.1
  98.5 0.1 eq.17
  98.6 1.4 fusion.28
  100.0 1.9 collective-permute-done.1
  101.9 3.1 pad_maximum_fusion
  105.0 6.8 %gather_fusion.2 = bf16[48,128,512]{2,1,0:T(8,128)(2,1)} fusion(bf16[24,128,512]{2,1,0:T(8,128)(2,1)} %bitcast.50, s32[1024]{0:T(1024)S(1)} %pad_clamp_fusion), kind=kCustom, calls=%fused_computation.2 | custom fusion | bytes 12583104 | tf_op jit(solution)/shard_map/gather | solution.py:67
  111.9 4.0 fusion.5
  115.9 1.7 convert_reduce_fusion.1
  117.7 0.5 fusion.3
  118.1 1.9 fusion.6
  120.1 12.3 %fusion.27 = (bf16[24,128,512]{2,0,1:T(8,128)(2,1)S(1)}, f32[24,128,512]{2,0,1:T(8,128)S(1)}) fusion(f32[48,128,512]{2,1,0:T(8,128)S(1)} %bitcast.49, s32[48]{0:T(128)S(1)} %eq.17), kind=kOutput, calls=%fused_computation.56 | convolution fusion | flops 907543680 | bytes 22020288 | tf_op jit(solution)/shard_map/en,nbf->ebf/dot_general | solution.py:97
  132.4 0.4 fusion.25
  132.8 0.1 copy.31
  132.9 9.1 %collective-permute-start.2 = (bf16[512,512]{1,0:T(8,128)(2,1)S(1)}, bf16[512,512]{1,0:T(8,128)(2,1)S(1)}, u32[]{:S(2)}, u32[]{:S(2)}) collective-permute-start(bf16[512,512]{1,0:T(8,128)(2,1)S(1)} %bitcast.54), channel_id=1, source_target_pairs={{0,4},{4,8},{8,12},{12,16},{16,20},{20,24},{24,28},{28,32},{32,36}... | collective-permute-start | bytes 1572872 | tf_op jit(solution)/shard_map/ppermute | solution.py:12
  142.0 0.1 copy.32
  142.1 1.3 collective-permute-start.3
  143.4 1.0 slice.78
  144.5 0.3 slice.79
  144.7 4.4 copy.29
  149.1 0.3 copy.30
  149.5 1.1 constant_dynamic-update-slice_fusion
  150.6 2.4 fusion.12
  153.1 1.4 fusion.31
  154.6 1.4 fusion.30
  156.0 83.0 %psum.23 = f32[512]{0:T(512)} all-reduce(f32[512]{0:T(512)S(1)} %get-tuple-element.33), channel_id=1, replica_groups=mesh['dom'=64,'rep'=4] {'dom','rep'}, use_global_device_ids=true, to_apply=%region_7.8 | all-reduce | flops 512 | bytes 4096 | tf_op jit(solution)/shard_map/psum | solution.py:78
  239.0 0.5 fusion.29
  239.5 2.2 add_convert_fusion
  241.7 234.0 %all-reduce.3.cloned.1.call-done = (f32[512,512]{1,0:T(8,128)}, f32[512,512]{1,0:T(8,128)}) async-done(((f32[512,512]{1,0:T(8,128)}, f32[512,512]{1,0:T(8,128)}), (f32[512,512]{1,0:T(8,128)}, f32[512,512]{1,0:T(8,128)})) %all-reduce.3.cloned.1.call-update) | async-done | bytes 2097168 | tf_op jit(solution)/shard_map/psum | solution.py:78
  475.6 2.3 copy.44
  477.9 2.3 copy.45
  (44 shorter events, 0.3 us)
Async XLA Ops:
  7.2 108.7 %copy-start = (bf16[512,512]{1,0:T(8,128)(2,1)S(1)}, bf16[512,512]{1,0:T(8,128)(2,1)}, u32[]{:S(2)}) copy-start(bf16[512,512]{1,0:T(8,128)(2,1)} %param.19) | copy-start | bytes 1572868
  7.2 20.9 %copy-start.1 = (bf16[512,512]{1,0:T(8,128)(2,1)S(1)}, bf16[512,512]{1,0:T(8,128)(2,1)}, u32[]{:S(2)}) copy-start(bf16[512,512]{1,0:T(8,128)(2,1)} %param.13) | copy-start | bytes 1572868
  15.3 47.4 %copy-start.10 = (s32[4,12]{1,0:T(4,128)S(1)}, s32[4,12]{1,0:T(4,128)}, u32[]{:S(2)}) copy-start(s32[4,12]{1,0:T(4,128)} %param.16) | copy-start | bytes 580
  15.3 47.5 %copy-start.9 = (s32[4,12]{1,0:T(4,128)S(1)}, s32[4,12]{1,0:T(4,128)}, u32[]{:S(2)}) copy-start(s32[4,12]{1,0:T(4,128)} %param.17) | copy-start | bytes 580
  15.3 47.5 %copy-start.3 = (bf16[4,12,128,128]{3,2,1,0:T(8,128)(2,1)S(1)}, bf16[4,12,128,128]{3,2,1,0:T(8,128)(2,1)}, u32[]{:S(2)}) copy-start(bf16[4,12,128,128]{3,2,1,0:T(8,128)(2,1)} %param.15) | copy-start | bytes 4718596
  16.0 21.5 %all-to-all-start = ((s32[64,8,1]{1,2,0:T(1,128)}), s32[64,8,1]{1,2,0:T(1,128)S(1)}, u32[]{:S(2)}, u32[]{:S(2)}) async-start(s32[64,8,1]{1,2,0:T(1,128)} %bitcast), calls=%async_computation | async-start | bytes 65536 | tf_op jit(solution)/shard_map/all_to_all | solution.py:58
  30.7 67.8 %copy-start.4 = (bf16[512,512]{1,0:T(8,128)(2,1)S(1)}, bf16[512,512]{1,0:T(8,128)(2,1)}, u32[]{:S(2)}) copy-start(bf16[512,512]{1,0:T(8,128)(2,1)} %param.18) | copy-start | bytes 1572868
  37.5 21.8 %all-to-all-start.1 = ((bf16[64,8,512]{2,1,0:T(8,128)(2,1)}), bf16[64,8,512]{2,1,0:T(8,128)(2,1)S(1)}, u32[]{:S(2)}, u32[]{:S(2)}) async-start(bf16[64,8,512]{2,1,0:T(8,128)(2,1)} %bitcast.2), calls=%async_computation.1 | async-start | bytes 1048576 | tf_op jit(solution)/shard_map/all_to_all | solution.py:57
  42.2 50.2 %all-gather.2.cloned.1.call-start = ((), (), s32[]{:S(2)}) async-start(), calls=%async_computation.3 | async-start | bytes 2621440 | tf_op jit(solution)/shard_map/all_gather | solution.py:65
  62.5 36.0 %copy-start.2 = (bf16[512,512]{1,0:T(8,128)(2,1)S(1)}, bf16[512,512]{1,0:T(8,128)(2,1)}, u32[]{:S(2)}) copy-start(bf16[512,512]{1,0:T(8,128)(2,1)} %scatter_custom_fusion) | copy-start | bytes 1572868
  62.6 176.9 %reduce-scatter.2.cloned.1.call-start = ((), (), s32[]{:S(2)}) async-start(), calls=%async_computation.4 | async-start | bytes 5242880 | tf_op jit(solution)/shard_map/reduce_scatter | solution.py:106
  94.6 5.3 %collective-permute-start = (bf16[512,512]{1,0:T(8,128)(2,1)}, bf16[512,512]{1,0:T(8,128)(2,1)}, u32[]{:S(2)}, u32[]{:S(2)}) collective-permute-start(bf16[512,512]{1,0:T(8,128)(2,1)} %get-tuple-element.39), channel_id=1, source_target_pairs={{0,4},{4,8},{8,12},{12,16},{16,20},{20,24},{24,28},{28,32},{32,36}... | collective-permute-start | bytes 1572872 | tf_op jit(solution)/shard_map/ppermute | solution.py:20
  97.2 4.7 collective-permute-start.1
  111.8 4.1 copy-start.6
  111.9 4.1 copy-start.11
  111.9 4.1 copy-start.12
  115.9 2.3 copy-start.7
  132.9 16.5 %collective-permute-start.2 = (bf16[512,512]{1,0:T(8,128)(2,1)S(1)}, bf16[512,512]{1,0:T(8,128)(2,1)S(1)}, u32[]{:S(2)}, u32[]{:S(2)}) collective-permute-start(bf16[512,512]{1,0:T(8,128)(2,1)S(1)} %bitcast.54), channel_id=1, source_target_pairs={{0,4},{4,8},{8,12},{12,16},{16,20},{20,24},{24,28},{28,32},{32,36}... | collective-permute-start | bytes 1572872 | tf_op jit(solution)/shard_map/ppermute | solution.py:12
  142.1 8.5 %collective-permute-start.3 = (bf16[512,512]{1,0:T(8,128)(2,1)S(1)}, bf16[512,512]{1,0:T(8,128)(2,1)S(1)}, u32[]{:S(2)}, u32[]{:S(2)}) collective-permute-start(bf16[512,512]{1,0:T(8,128)(2,1)S(1)} %bitcast.53), channel_id=1, source_target_pairs={{4,0},{8,4},{12,8},{16,12},{20,16},{24,20},{28,24},{32,28},{36,32}... | collective-permute-start | bytes 1572872 | tf_op jit(solution)/shard_map/ppermute | solution.py:12
  149.5 3.7 copy-start.8
  153.1 85.9 %copy-start.5 = (bf16[512,512]{1,0:T(8,128)(2,1)S(1)}, bf16[512,512]{1,0:T(8,128)(2,1)}, u32[]{:S(2)}) copy-start(bf16[512,512]{1,0:T(8,128)(2,1)} %param.18) | copy-start | bytes 1572868
  153.1 322.6 %all-reduce.3.cloned.1.call-start = ((), (), s32[]{:S(2)}) async-start(), calls=%async_computation.5 | async-start | bytes 4194304 | tf_op jit(solution)/shard_map/psum | solution.py:78
Sparse Core Ops, SparseCore 0:
  62.7 29.6 all-gather.1
  153.2 52.8 reduce-scatter.1
  213.1 262.4 all-reduce.2
where the time goes:
time: 487 us
  waiting for transfers between devices  288 us (59%)
  blocking collectives  83 us (17%)
  local copies, waits for them, and re-layouts  31.1 us (6%)
  starting transfers between devices  31.1 us (6%)
  matrix products  25.2 us (5%)
  other arithmetic  14.6 us (3%)
  between operations  14.1 us (3%)
    psum x1, waiting for transfers between devices, shards(): lax.psum((contract_rows(features, dz), contract_rows(agg, dz), jnp.sum(dz...  234 us
    psum x1, blocking collectives, shards(): lax.psum((contract_rows(features, dz), contract_rows(agg, dz), jnp.sum(dz...  83 us
    all_gather x1, waiting for transfers between devices, shards(): whole = lax.all_gather(features, 'rep', axis=0, tiled=True)  29.2 us
    all_to_all x1, waiting for transfers between devices, shards(): lax.all_to_all(x_loader[order], 'dom', split_axis=0, concat_axis=0, tiled...  15.8 us
    dot_general x1, matrix products, shards(): jnp.einsum('en,nbf->ebf', selector, terms.reshape(-1, 128, width), precis...  12.3 us
    all_to_all x1, starting transfers between devices, shards(): lax.all_to_all((owner_index % rows)[order], 'dom', split_axis=0, concat_a...  12.1 us
    ppermute x2, starting transfers between devices, shifted(): lax.ppermute(value, axis, [(source, source + steps) for source in range(f...  10.4 us
  transfers between devices with their start and end apart: 9, of which 5 were waited for; matrix products, arithmetic and copies ran while one was open for 4% of the time, Pallas kernels for 0%

commit v1 on v0

--- a/solution.py
+++ b/solution.py
@@ -62,7 +62,12 @@
     local_cols = tile_cols - first_tile
     masked = tile_vals * tile_live.astype(jnp.bfloat16)[:, :, None, None]
     degree = 1.0 + jnp.sum(masked, axis=(1, 3), dtype=jnp.float32)
-    whole = lax.all_gather(features, "rep", axis=0, tiled=True)
+    ring = [features]
+    for hop in range(3):
+        ring.append(lax.ppermute(ring[-1], "rep", [(dev, (dev + 1) % 4) for dev in range(4)]))
+    whole = jnp.roll(
+        jnp.concatenate(ring[::-1], axis=0), (lax.axis_index("rep") + 1) * ring[0].shape[0], axis=0
+    )
     extended = with_halo(whole, (("dom", 0),), rim_rows)
     picked = extended.reshape(-1, 128, width)[local_cols]
     summed = jnp.einsum("tkab,tkbf->taf", masked, picked, preferred_element_type=jnp.float32)

time: 487 us -> 465 us (0.955)
  waiting for transfers between devices: 288 us -> 258 us
    ppermute x0 -> x3, waiting for transfers between devices: none -> 35.6 us  [shards(): lax.ppermute(ring[-1], 'rep', [(dev, (dev + 1) % 4) for dev in range(4)])]
    psum x1, waiting for transfers between devices: 234 us -> 198 us  [shards(): lax.psum((contract_rows(features, dz), contract_rows(agg, dz), jnp.sum(dz...]
    all_gather x1 -> x0, waiting for transfers between devices: 29.2 us -> none  [shards(): whole = lax.all_gather(features, 'rep', axis=0, tiled=True)]
  transfers between devices with their start and end apart: 9 -> 11, of which waited for: 5 -> 7; matrix products, arithmetic and copies ran while one was open for 4% -> 4% of each run, Pallas kernels for 0% -> 0%
where the time goes in v1:
time: 465 us; the launch traced here: 464 us
  waiting for transfers between devices  258 us (55%)
  blocking collectives  86.1 us (19%)
  starting transfers between devices  34.4 us (7%)
  local copies, waits for them, and re-layouts  31.3 us (7%)
  matrix products  25.2 us (5%)
  between operations  15.9 us (3%)
  other arithmetic  13.3 us (3%)
    psum x1, waiting for transfers between devices, shards(): lax.psum((contract_rows(features, dz), contract_rows(agg, dz), jnp.sum(dz...  198 us
    psum x1, blocking collectives, shards(): lax.psum((contract_rows(features, dz), contract_rows(agg, dz), jnp.sum(dz...  86.1 us
    ppermute x3, waiting for transfers between devices, shards(): lax.ppermute(ring[-1], 'rep', [(dev, (dev + 1) % 4) for dev in range(4)])  35.6 us
    all_to_all x1, waiting for transfers between devices, shards(): lax.all_to_all(x_loader[order], 'dom', split_axis=0, concat_axis=0, tiled...  15.8 us
    dot_general x1, matrix products, shards(): jnp.einsum('en,nbf->ebf', selector, terms.reshape(-1, 128, width), precis...  12.3 us
    all_to_all x1, starting transfers between devices, shards(): lax.all_to_all((owner_index % rows)[order], 'dom', split_axis=0, concat_a...  12.1 us
    ppermute x2, starting transfers between devices, shifted(): lax.ppermute(value, axis, [(source, source + steps) for source in range(f...  10.4 us
  transfers between devices with their start and end apart: 11, of which 7 were waited for; matrix products, arithmetic and copies ran while one was open for 4% of the time, Pallas kernels for 0%

profile of v1, /device:TPU:2, one launch (start us, length us, event | category | flops | bytes accessed | tf_op | source)
XLA Modules:
  0.0 464.4 jit_solution(15698030069344955255)
XLA Ops:
  8.0 0.8 add_select_fusion
  8.8 3.8 sort.17
  12.6 3.5 gather_fusion
  16.1 0.7 all_to_all.16
  16.8 12.1 %all-to-all-start = ((s32[64,8,1]{1,2,0:T(1,128)}), s32[64,8,1]{1,2,0:T(1,128)S(1)}, u32[]{:S(2)}, u32[]{:S(2)}) async-start(s32[64,8,1]{1,2,0:T(1,128)} %bitcast), calls=%async_computation | async-start | bytes 65536 | tf_op jit(solution)/shard_map/all_to_all | solution.py:58
  28.9 2.6 gather_fusion.1
  31.6 6.8 %all-to-all-done = s32[64,8,1]{1,2,0:T(1,128)S(1)} async-done(((s32[64,8,1]{1,2,0:T(1,128)}), s32[64,8,1]{1,2,0:T(1,128)S(1)}, u32[]{:S(2)}, u32[]{:S(2)}) %all-to-all-start) | async-done | bytes 2080 | tf_op jit(solution)/shard_map/all_to_all | solution.py:58
  38.4 4.6 all-to-all-start.1
  43.1 0.5 broadcast.97
  43.6 0.7 reduce.7
  44.4 15.8 %all-to-all-done.1 = bf16[64,8,512]{2,1,0:T(8,128)(2,1)S(1)} async-done(((bf16[64,8,512]{2,1,0:T(8,128)(2,1)}), bf16[64,8,512]{2,1,0:T(8,128)(2,1)S(1)}, u32[]{:S(2)}, u32[]{:S(2)}) %all-to-all-start.1) | async-done | bytes 524320 | tf_op jit(solution)/shard_map/all_to_all | solution.py:57
  60.2 2.5 scatter_custom_fusion
  62.7 1.6 collective-permute-start
  64.3 12.5 %collective-permute-done = bf16[512,512]{1,0:T(8,128)(2,1)S(1)} collective-permute-done((bf16[512,512]{1,0:T(8,128)(2,1)S(1)}, bf16[512,512]{1,0:T(8,128)(2,1)S(1)}, u32[]{:S(2)}, u32[]{:S(2)}) %collective-permute-start) | collective-permute-done | bytes 524320 | tf_op jit(solution)/shard_map/ppermute | solution.py:67
  76.7 1.5 collective-permute-start.1
  78.4 11.5 %collective-permute-done.1 = bf16[512,512]{1,0:T(8,128)(2,1)} collective-permute-done((bf16[512,512]{1,0:T(8,128)(2,1)S(1)}, bf16[512,512]{1,0:T(8,128)(2,1)}, u32[]{:S(2)}, u32[]{:S(2)}) %collective-permute-start.1) | collective-permute-done | bytes 524320 | tf_op jit(solution)/shard_map/ppermute | solution.py:67
  90.0 1.5 collective-permute-start.2
  91.5 0.5 convert_reduce_fusion
  91.9 11.6 %collective-permute-done.2 = bf16[512,512]{1,0:T(8,128)(2,1)S(1)} collective-permute-done((bf16[512,512]{1,0:T(8,128)(2,1)}, bf16[512,512]{1,0:T(8,128)(2,1)S(1)}, u32[]{:S(2)}, u32[]{:S(2)}) %collective-permute-start.2) | collective-permute-done | bytes 524320 | tf_op jit(solution)/shard_map/ppermute | solution.py:67
  103.6 1.1 constant_dynamic-update-slice_fusion.6
  104.8 1.1 constant_dynamic-update-slice_fusion.2
  106.3 1.3 collective-permute-start.3
  107.6 1.3 collective-permute-start.4
  108.9 1.4 fusion.27
  110.3 0.5 constant_dynamic-slice_fusion.2
  110.9 1.4 collective-permute-done.4
  112.3 1.8 pad_maximum_fusion
  114.1 6.8 %gather_fusion.2 = bf16[48,128,512]{2,1,0:T(8,128)(2,1)} fusion(bf16[24,128,512]{2,1,0:T(8,128)(2,1)} %bitcast.50, s32[1024]{0:T(1024)S(1)} %pad_clamp_fusion), kind=kCustom, calls=%fused_computation.2 | custom fusion | bytes 12583104 | tf_op jit(solution)/shard_map/gather | solution.py:72
  120.9 4.0 fusion.5
  125.0 1.7 convert_reduce_fusion.1
  126.7 0.5 fusion.3
  127.2 1.9 fusion.6
  129.1 12.3 %fusion.26 = (bf16[24,128,512]{2,0,1:T(8,128)(2,1)S(1)}, f32[24,128,512]{2,0,1:T(8,128)S(1)}) fusion(f32[48,128,512]{2,1,0:T(8,128)S(1)} %bitcast.49, s32[48]{0:T(128)S(1)} %eq.20), kind=kOutput, calls=%fused_computation.66 | convolution fusion | flops 907543680 | bytes 22020288 | tf_op jit(solution)/shard_map/en,nbf->ebf/dot_general | solution.py:102
  141.5 0.4 fusion.25
  142.0 9.1 %collective-permute-start.5 = (bf16[512,512]{1,0:T(8,128)(2,1)S(1)}, bf16[512,512]{1,0:T(8,128)(2,1)S(1)}, u32[]{:S(2)}, u32[]{:S(2)}) collective-permute-start(bf16[512,512]{1,0:T(8,128)(2,1)S(1)} %bitcast.54), channel_id=1, source_target_pairs={{0,4},{4,8},{8,12},{12,16},{16,20},{20,24},{24,28},{28,32},{32,36}... | collective-permute-start | bytes 1572872 | tf_op jit(solution)/shard_map/ppermute | solution.py:12
  151.2 1.3 collective-permute-start.6
  152.5 1.0 slice.76
  153.8 4.4 copy.29
  158.6 1.1 constant_dynamic-update-slice_fusion.8
  159.7 2.4 fusion.12
  162.2 1.4 fusion.30
  163.7 1.4 fusion.29
  165.1 86.1 %psum.23 = f32[512]{0:T(512)} all-reduce(f32[512]{0:T(512)S(1)} %get-tuple-element.33), channel_id=1, replica_groups=mesh['dom'=64,'rep'=4] {'dom','rep'}, use_global_device_ids=true, to_apply=%region_7.8 | all-reduce | flops 512 | bytes 4096 | tf_op jit(solution)/shard_map/psum | solution.py:83
  251.3 0.5 fusion.28
  251.8 2.2 add_convert_fusion
  253.9 198.5 %all-reduce.3.cloned.1.call-done = (f32[512,512]{1,0:T(8,128)}, f32[512,512]{1,0:T(8,128)}) async-done(((f32[512,512]{1,0:T(8,128)}, f32[512,512]{1,0:T(8,128)}), (f32[512,512]{1,0:T(8,128)}, f32[512,512]{1,0:T(8,128)})) %all-reduce.3.cloned.1.call-update) | async-done | bytes 2097168 | tf_op jit(solution)/shard_map/psum | solution.py:83
  452.4 2.3 copy.51
  454.7 2.3 copy.52
  (56 shorter events, 1.8 us)
Async XLA Ops:
  8.0 117.0 %copy-start = (bf16[512,512]{1,0:T(8,128)(2,1)S(1)}, bf16[512,512]{1,0:T(8,128)(2,1)}, u32[]{:S(2)}) copy-start(bf16[512,512]{1,0:T(8,128)(2,1)} %param.19) | copy-start | bytes 1572868
  8.0 20.9 %copy-start.2 = (bf16[512,512]{1,0:T(8,128)(2,1)S(1)}, bf16[512,512]{1,0:T(8,128)(2,1)}, u32[]{:S(2)}) copy-start(bf16[512,512]{1,0:T(8,128)(2,1)} %param.13) | copy-start | bytes 1572868
  12.6 65.7 %copy-start.10 = (s32[4,12]{1,0:T(4,128)S(1)}, s32[4,12]{1,0:T(4,128)}, u32[]{:S(2)}) copy-start(s32[4,12]{1,0:T(4,128)} %param.16) | copy-start | bytes 580
  12.6 65.7 %copy-start.9 = (s32[4,12]{1,0:T(4,128)S(1)}, s32[4,12]{1,0:T(4,128)}, u32[]{:S(2)}) copy-start(s32[4,12]{1,0:T(4,128)} %param.17) | copy-start | bytes 580
  12.6 78.8 %copy-start.3 = (bf16[4,12,128,128]{3,2,1,0:T(8,128)(2,1)S(1)}, bf16[4,12,128,128]{3,2,1,0:T(8,128)(2,1)}, u32[]{:S(2)}) copy-start(bf16[4,12,128,128]{3,2,1,0:T(8,128)(2,1)} %param.15) | copy-start | bytes 4718596
  16.8 21.5 %all-to-all-start = ((s32[64,8,1]{1,2,0:T(1,128)}), s32[64,8,1]{1,2,0:T(1,128)S(1)}, u32[]{:S(2)}, u32[]{:S(2)}) async-start(s32[64,8,1]{1,2,0:T(1,128)} %bitcast), calls=%async_computation | async-start | bytes 65536 | tf_op jit(solution)/shard_map/all_to_all | solution.py:58
  38.4 21.8 %all-to-all-start.1 = ((bf16[64,8,512]{2,1,0:T(8,128)(2,1)}), bf16[64,8,512]{2,1,0:T(8,128)(2,1)S(1)}, u32[]{:S(2)}, u32[]{:S(2)}) async-start(bf16[64,8,512]{2,1,0:T(8,128)(2,1)} %bitcast.2), calls=%async_computation.1 | async-start | bytes 1048576 | tf_op jit(solution)/shard_map/all_to_all | solution.py:57
  43.0 208.8 %reduce-scatter.2.cloned.1.call-start = ((), (), s32[]{:S(2)}) async-start(), calls=%async_computation.3 | async-start | bytes 5242880 | tf_op jit(solution)/shard_map/reduce_scatter | solution.py:111
  62.7 14.0 %collective-permute-start = (bf16[512,512]{1,0:T(8,128)(2,1)S(1)}, bf16[512,512]{1,0:T(8,128)(2,1)S(1)}, u32[]{:S(2)}, u32[]{:S(2)}) collective-permute-start(bf16[512,512]{1,0:T(8,128)(2,1)S(1)} %scatter_custom_fusion), channel_id=1, source_target_pairs={{0,1},{1,2},{2,3},{3,0},{4,5},{5,6},{6,7},{7,4},{8,9},{9,10},{10,1... | collective-permute-start | bytes 1572872 | tf_op jit(solution)/shard_map/ppermute | solution.py:67
  76.7 13.2 %collective-permute-start.1 = (bf16[512,512]{1,0:T(8,128)(2,1)S(1)}, bf16[512,512]{1,0:T(8,128)(2,1)}, u32[]{:S(2)}, u32[]{:S(2)}) collective-permute-start(bf16[512,512]{1,0:T(8,128)(2,1)S(1)} %collective-permute-done), channel_id=1, source_target_pairs={{0,1},{1,2},{2,3},{3,0},{4,5},{5,6},{6,7},{7,4},{8,9},{9,10},{10,1... | collective-permute-start | bytes 1572872 | tf_op jit(solution)/shard_map/ppermute | solution.py:67
  90.0 13.6 %collective-permute-start.2 = (bf16[512,512]{1,0:T(8,128)(2,1)}, bf16[512,512]{1,0:T(8,128)(2,1)S(1)}, u32[]{:S(2)}, u32[]{:S(2)}) collective-permute-start(bf16[512,512]{1,0:T(8,128)(2,1)} %collective-permute-done.1), channel_id=1, source_target_pairs={{0,1},{1,2},{2,3},{3,0},{4,5},{5,6},{6,7},{7,4},{8,9},{9,10},{10,1... | collective-permute-start | bytes 1572872 | tf_op jit(solution)/shard_map/ppermute | solution.py:67
  104.7 4.2 copy-start.4
  106.3 4.6 collective-permute-start.3
  107.6 4.6 collective-permute-start.4
  120.9 4.1 copy-start.6
  120.9 4.1 copy-start.11
  120.9 4.1 copy-start.12
  124.9 2.3 copy-start.7
  142.0 16.6 %collective-permute-start.5 = (bf16[512,512]{1,0:T(8,128)(2,1)S(1)}, bf16[512,512]{1,0:T(8,128)(2,1)S(1)}, u32[]{:S(2)}, u32[]{:S(2)}) collective-permute-start(bf16[512,512]{1,0:T(8,128)(2,1)S(1)} %bitcast.54), channel_id=1, source_target_pairs={{0,4},{4,8},{8,12},{12,16},{16,20},{20,24},{24,28},{28,32},{32,36}... | collective-permute-start | bytes 1572872 | tf_op jit(solution)/shard_map/ppermute | solution.py:12
  151.2 8.5 %collective-permute-start.6 = (bf16[512,512]{1,0:T(8,128)(2,1)S(1)}, bf16[512,512]{1,0:T(8,128)(2,1)S(1)}, u32[]{:S(2)}, u32[]{:S(2)}) collective-permute-start(bf16[512,512]{1,0:T(8,128)(2,1)S(1)} %bitcast.53), channel_id=1, source_target_pairs={{4,0},{8,4},{12,8},{16,12},{20,16},{24,20},{28,24},{32,28},{36,32}... | collective-permute-start | bytes 1572872 | tf_op jit(solution)/shard_map/ppermute | solution.py:12
  159.7 2.5 copy-start.8
  162.2 89.1 %copy-start.5 = (bf16[512,512]{1,0:T(8,128)(2,1)S(1)}, bf16[512,512]{1,0:T(8,128)(2,1)}, u32[]{:S(2)}) copy-start(bf16[512,512]{1,0:T(8,128)(2,1)} %param.18) | copy-start | bytes 1572868
  162.2 290.2 %all-reduce.3.cloned.1.call-start = ((), (), s32[]{:S(2)}) async-start(), calls=%async_computation.4 | async-start | bytes 4194304 | tf_op jit(solution)/shard_map/psum | solution.py:83
  165.1 291.8 %copy-start.1 = (bf16[512,512]{1,0:T(8,128)(2,1)S(1)}, bf16[512,512]{1,0:T(8,128)(2,1)}, u32[]{:S(2)}) copy-start(bf16[512,512]{1,0:T(8,128)(2,1)} %param.19) | copy-start | bytes 1572868
Sparse Core Ops, SparseCore 0:
  162.3 55.4 reduce-scatter.1
Sparse Core Ops, SparseCore 1:
  169.7 282.7 all-reduce.2
